TPU v7x, 512 devices: a whole 4x8x8 slice. The times are simulated.
512 devices in a mesh: grp: 16 (over z, core), tok: 32 (over y, x).
Axes of the slice: x: 4, y: 8, z: 8, core: 2. Of those that a mesh axis runs over, the one named last changes fastest.
Arguments:
- patches: bfloat16 [32, 256, 1664], P('tok', 'grp'), may hold values from -54 to 54
- segment_ids: int32 [32, 256], P('tok'), may hold values from 0 to 32, as said below
- padding: int32 [32, 256], P('tok'), may hold values from 0 to 1, as said below
- request_owner: int32 [32, 32], P('tok'), may hold values from 0 to 31, as said below
- first_gain: float32 [1664], replicated, may hold values from 0.5 to 1.5
- first_shift: float32 [1664], replicated, may hold values from -3 to 3
- input_weight: bfloat16 [1664, 16, 312], P(None, 'grp'), may hold values from -0.15625 to 0.15625
- input_shift: float32 [16, 312], P('grp'), may hold values from -40 to 40
- output_weight: bfloat16 [16, 104, 1664], P('grp'), may hold values from -0.15625 to 0.15625
- output_shift: float32 [1664], replicated, may hold values from -3 to 3
- second_gain: float32 [1664], replicated, may hold values from 0.5 to 1.5
- second_shift: float32 [1664], replicated, may hold values from -3 to 3
- up_weight: bfloat16 [1664, 4096], P(None, 'grp'), may hold values from -0.15625 to 0.15625
- up_shift: float32 [4096], P('grp'), may hold values from -3 to 3
- down_weight: bfloat16 [4096, 1664], P('grp'), may hold values from -0.09375 to 0.09375
- down_shift: float32 [1664], replicated, may hold values from -3 to 3
- merge_weight: bfloat16 [6656, 1664], P(None, 'grp'), may hold values from -0.078125 to 0.078125
- merge_shift: float32 [1664], P('grp'), may hold values from -3 to 3
Outputs:
- routed: bfloat16 [32, 32, 8, 1664], P('tok', None, None, 'grp')
Inputs may be any that keep to these rules, and one draw needn't show every extreme that they name: `segment_ids`: patches come in aligned runs of four with one id (a 2x2 window); ids never fall along a group; an image spans 1 to 8 windows; every group holds an image of exactly 8 windows; padding stands at the end of a group and carries the id 32. `padding`: 0 exactly where segment_ids is 32. `request_owner`: every row is a permutation of 0 to 31; in every draw one owner receives an image of 8 windows from every group.
All inputs are finite; a program needn't handle non-finite values.
Results may differ from a plain program's by a relative error of at most 0.02.
The roundings to bfloat16 on the way count: a program that leaves them out, or rounds other values in their place, can miss the bound.
Values may be sent and summed in bfloat16 or wider, within the bound.
No kernel may reach another device: no remote copies, remote signals or barrier semaphores. Data moves between devices by JAX's collectives and lax.ppermute only.
A program may use at most 64 MiB of HBM per device.

v0:
```python
import jax
import jax.numpy as jnp
from jax import lax
from jax.sharding import PartitionSpec as P

CAP = 8


epsilon = 1e-06


def normalize(stream, factor, adjust):
    average = jnp.mean(stream, axis=-1, keepdims=True)
    centered = stream - average
    variance = jnp.mean(centered * centered, axis=-1, keepdims=True)
    return centered * lax.rsqrt(variance + epsilon) * factor + adjust


def attention_mask(segments, live_rows):
    count = segments.shape[0]
    same_image = segments[:, None] == segments[None, :]
    allowed = jnp.logical_and(same_image, live_rows[None, :] == 1)
    diagonal = jnp.arange(count)[:, None] == jnp.arange(count)[None, :]
    return jnp.logical_or(allowed, diagonal)


def softmax_rows(scores, allowed):
    masked = jnp.where(allowed, scores, -jnp.inf)
    row_max = jnp.max(masked, axis=-1, keepdims=True)
    powered = jnp.where(allowed, jnp.exp(masked - row_max), 0.0)
    return powered / jnp.sum(powered, axis=-1, keepdims=True)


def attend(projected, segments, live_rows, head_dim):
    queries = projected[:, :, :head_dim]
    key_rows = projected[:, :, head_dim : 2 * head_dim]
    value_rows = projected[:, :, 2 * head_dim :]
    scores = jnp.einsum(
        "qhe,khe->hqk", queries, key_rows, preferred_element_type=jnp.float32
    ) * head_dim ** (-0.5)
    probabilities = softmax_rows(scores, attention_mask(segments, live_rows)[None]).astype(
        jnp.bfloat16
    )
    return jnp.einsum(
        "hqk,khe->qhe", probabilities, value_rows, preferred_element_type=jnp.float32
    ).astype(jnp.bfloat16)


def routed_rows(merged, segments, live_rows, owners):
    window_segments = segments[::4]
    window_live = live_rows[::4]
    window_count = window_segments.shape[0]
    places = jnp.arange(window_count)
    earlier = jnp.logical_and(
        window_segments[None, :] == window_segments[:, None], places[None, :] < places[:, None]
    )
    slot_index = jnp.sum(earlier.astype(jnp.int32), axis=1)
    groups = owners.shape[0]
    matched = (jnp.arange(groups)[None, :] == window_segments[:, None]).astype(jnp.int32)
    owner_of = jnp.sum(matched * owners[None, :], axis=1)
    target = owner_of * CAP + slot_index
    one_hot = jnp.logical_and(
        target[:, None] == jnp.arange(groups * CAP)[None, :], window_live[:, None] == 1
    )
    outgoing = jnp.einsum(
        "wc,wd->cd", one_hot.astype(jnp.bfloat16), merged, preferred_element_type=jnp.float32
    )
    return outgoing.astype(jnp.bfloat16).reshape(groups, CAP, merged.shape[1])


def on_device(
    patches,
    segment_ids,
    padding,
    request_owner,
    first_gain,
    first_shift,
    input_weight,
    input_shift,
    output_weight,
    output_shift,
    second_gain,
    second_shift,
    up_weight,
    up_shift,
    down_weight,
    down_shift,
    merge_weight,
    merge_shift,
):
    row_count = patches.shape[1]
    model_width = patches.shape[2]
    head_dim = input_weight.shape[2] // 3
    segments = segment_ids[0]
    live_rows = padding[0]
    stream = patches[0]
    normed = normalize(stream.astype(jnp.float32), first_gain, first_shift).astype(jnp.bfloat16)
    lifted = jnp.einsum(
        "sd,dhe->she",
        lax.all_gather(normed, "grp", axis=0, tiled=True),
        input_weight,
        preferred_element_type=jnp.float32,
    )
    projected = (lifted + input_shift[None]).astype(jnp.bfloat16)
    mixed = attend(projected, segments, live_rows, head_dim)
    block = mixed
    attended = lax.psum_scatter(
        jnp.einsum("qhe,hed->qd", block, output_weight, preferred_element_type=jnp.float32).astype(
            jnp.bfloat16
        ),
        "grp",
        scatter_dimension=0,
        tiled=True,
    ).astype(jnp.float32)
    residual = (stream.astype(jnp.float32) + attended + output_shift).astype(jnp.bfloat16)
    normed_again = normalize(residual.astype(jnp.float32), second_gain, second_shift).astype(
        jnp.bfloat16
    )
    lifted = (
        jnp.dot(
            lax.all_gather(normed_again, "grp", axis=0, tiled=True),
            up_weight,
            preferred_element_type=jnp.float32,
        )
        + up_shift
    )
    activated = jax.nn.gelu(lifted, approximate=False).astype(jnp.bfloat16)
    block = activated
    fed = lax.psum_scatter(
        jnp.dot(block, down_weight, preferred_element_type=jnp.float32).astype(jnp.bfloat16),
        "grp",
        scatter_dimension=0,
        tiled=True,
    ).astype(jnp.float32)
    layer_out = (residual.astype(jnp.float32) + fed + down_shift).astype(jnp.bfloat16)
    windows = layer_out.reshape(row_count // 4, 4 * model_width)
    merged = (
        jnp.dot(
            lax.all_gather(windows, "grp", axis=0, tiled=True),
            merge_weight,
            preferred_element_type=jnp.float32,
        )
        + merge_shift
    ).astype(jnp.bfloat16)
    outgoing = routed_rows(merged, segments, live_rows, request_owner[0])
    delivered = lax.all_to_all(outgoing, "tok", split_axis=0, concat_axis=0, tiled=True)
    return delivered[None]


def solution(mesh):
    return jax.shard_map(
        on_device,
        mesh=mesh,
        in_specs=(
            P("tok", "grp", None),
            P("tok", None),
            P("tok", None),
            P("tok", None),
            P(),
            P(),
            P(None, "grp", None),
            P("grp", None),
            P("grp", None, None),
            P(),
            P(),
            P(),
            P(None, "grp"),
            P("grp"),
            P("grp", None),
            P(),
            P(None, "grp"),
            P("grp"),
        ),
        out_specs=P("tok", None, None, "grp"),
        check_vma=False,
    )
```

profile of v0, /device:TPU:1, one launch (start us, length us, event | category | flops | bytes accessed | tf_op | source)
XLA Modules:
  0.0 226.3 jit_solution(18325256107197689622)
XLA Ops:
  6.5 0.0 copy-start
  6.5 0.0 reduce-scatter.3.cloned.1.call-start
  6.5 1.0 convert_reduce_fusion.1
  7.6 1.0 fusion.68
  8.6 0.9 fusion.71
  9.5 0.0 copy-start.6
  9.5 26.8 %all_gather.9 = bf16[256,1664]{1,0:T(8,128)(2,1)S(1)} all-gather(bf16[16,1664]{1,0:T(8,128)(2,1)S(1)} %fusion.71), channel_id=1, replica_groups=mesh['grp'=16,'tok'=32] {'grp'}, dimensions={0}, use_global_device_ids=true | all-gather | bytes 905216 | tf_op jit(solution)/shard_map/all_gather | solution.py:100
  36.4 0.7 compare_reduce_fusion
  37.1 0.7 reduce.5
  37.8 0.0 copy-start.9
  37.8 1.8 fusion.2
  39.6 0.0 copy-done.6
  39.6 0.3 fusion.115
  39.8 0.2 fusion.18
  40.0 0.0 copy-done.9
  40.0 0.0 copy-start.1
  40.0 0.0 copy-start.2
  40.0 0.0 copy-start.3
  40.0 0.0 copy-start.4
  40.1 1.6 convolution_convert_fusion.1
  41.7 0.0 copy-start.8
  41.7 0.0 copy-start.10
  41.7 0.0 reduce-scatter.3.cloned.1.call-update
  41.7 0.0 reduce-scatter.5.cloned.1.call-start
  41.7 55.2 %reduce-scatter.3.cloned.1.call-done = bf16[16,1664]{1,0:T(8,128)(2,1)} async-done(((bf16[256,1664]{1,0:T(8,128)(2,1)}), bf16[16,1664]{1,0:T(8,128)(2,1)}) %reduce-scatter.3.cloned.1.call-update) | async-done | bytes 53264 | tf_op jit(solution)/shard_map/reduce_scatter | solution.py:107
  97.0 0.0 copy-done.1
  97.0 0.0 copy-done.2
  97.0 0.9 convert_reduce_fusion
  97.9 0.2 fusion.64
  98.1 0.0 copy-done.3
  98.1 0.0 copy-done.4
  98.1 0.1 fusion.67
  98.2 20.1 %all_gather.10 = bf16[256,1664]{1,0:T(8,128)(2,1)S(1)} all-gather(bf16[16,1664]{1,0:T(8,128)(2,1)S(1)} %fusion.67), channel_id=1, replica_groups=mesh['grp'=16,'tok'=32] {'grp'}, dimensions={0}, use_global_device_ids=true | all-gather | bytes 905216 | tf_op jit(solution)/shard_map/all_gather | solution.py:121
  118.3 0.0 copy-done.8
  118.3 0.0 copy-done.10
  118.3 0.0 copy-start.11
  118.3 0.0 copy-start.12
  118.3 0.0 copy-start.5
  118.3 3.9 %convolution_convert_fusion = bf16[256,1664]{1,0:T(8,128)(2,1)} fusion(bf16[256,1664]{1,0:T(8,128)(2,1)S(1)} %copy-done.8, bf16[256,1664]{1,0:T(8,128)(2,1)S(1)} %all_gather.10, bf16[1664,256]{1,0:T(8,128)(2,1)} %param.30, f32[256]{0:T(256)S(1)} %copy-done.10), kind=kOutput, calls=%fused_computation | convolution fusion | flops 440958976 | bytes 3408896 | tf_op jit(solution)/shard_map/dot_general | solution.py:130
  122.3 0.0 reduce-scatter.5.cloned.1.call-update
  122.3 0.2 slice.15
  122.4 0.0 copy-done.11
  122.4 0.2 slice.16
  122.6 0.2 convert_reduce_fusion.2
  122.8 0.0 copy-done.12
  122.8 0.1 select_reduce_fusion
  122.9 55.7 %reduce-scatter.5.cloned.1.call-done = bf16[16,1664]{1,0:T(8,128)(2,1)} async-done(((bf16[256,1664]{1,0:T(8,128)(2,1)}), bf16[16,1664]{1,0:T(8,128)(2,1)}) %reduce-scatter.5.cloned.1.call-update) | async-done | bytes 53264 | tf_op jit(solution)/shard_map/reduce_scatter | solution.py:129
  178.6 0.0 copy-done.5
  178.6 0.8 fusion.75
  179.4 0.0 copy-start.7
  179.5 20.1 %all-gather = bf16[16,4,6656]{2,1,0:T(4,128)(2,1)S(1)} all-gather(bf16[1,4,6656]{2,1,0:T(4,128)(2,1)S(1)} %reshape.104), channel_id=1, replica_groups=mesh['grp'=16,'tok'=32] {'grp'}, dimensions={0}, use_global_device_ids=true | all-gather | bytes 905216 | tf_op jit(solution)/shard_map/all_gather | solution.py:139
  199.5 0.2 reshape.105
  199.7 0.0 copy-done
  199.7 0.0 copy-done.7
  199.8 0.8 convolution_convert_fusion.2
  200.6 0.1 copy.26
  200.7 18.1 %all_to_all.5 = bf16[32,8,104]{2,1,0:T(8,128)(2,1)S(1)} all-to-all(bf16[32,8,104]{2,1,0:T(8,128)(2,1)S(1)} %bitcast.64), channel_id=1, replica_groups=mesh['grp'=16,'tok'=32] {'tok'}, dimensions={0} | all-to-all | bytes 106496 | tf_op jit(solution)/shard_map/all_to_all | solution.py:146
  218.8 0.6 copy.29
  (7 shorter events, 0.1 us)
Async XLA Ops:
  6.5 193.2 %copy-start = (bf16[6656,104]{0,1:T(8,128)(2,1)S(1)}, bf16[6656,104]{0,1:T(8,128)(2,1)}, u32[]{:S(2)}) copy-start(bf16[6656,104]{0,1:T(8,128)(2,1)} %param.34) | copy-start | bytes 4153348
  6.5 90.4 %reduce-scatter.3.cloned.1.call-start = ((), (), s32[]{:S(2)}) async-start(), calls=%async_computation.3 | async-start | bytes 905216 | tf_op jit(solution)/shard_map/reduce_scatter | solution.py:107
  9.5 30.0 %copy-start.6 = (s32[1,256]{1,0:T(1,128)S(1)}, s32[1,256]{1,0:T(1,128)}, u32[]{:S(2)}) copy-start(s32[1,256]{1,0:T(1,128)} %param.19) | copy-start | bytes 3076
  37.8 2.2 copy-start.9
  40.0 57.0 %copy-start.1 = (bf16[1,16,1664]{2,1,0:T(8,128)(2,1)S(1)}, bf16[1,16,1664]{2,1,0:T(8,128)(2,1)}, u32[]{:S(2)}) copy-start(bf16[1,16,1664]{2,1,0:T(8,128)(2,1)} %param.18) | copy-start | bytes 159748
  40.0 57.0 %copy-start.2 = (f32[1664]{0:T(1024)S(1)}, f32[1664]{0:T(1024)}, u32[]{:S(2)}) copy-start(f32[1664]{0:T(1024)} %param.27) | copy-start | bytes 19972
  40.0 58.1 %copy-start.3 = (f32[1664]{0:T(1024)S(1)}, f32[1664]{0:T(1024)}, u32[]{:S(2)}) copy-start(f32[1664]{0:T(1024)} %param.29) | copy-start | bytes 19972
  40.0 58.1 %copy-start.4 = (f32[1664]{0:T(1024)S(1)}, f32[1664]{0:T(1024)}, u32[]{:S(2)}) copy-start(f32[1664]{0:T(1024)} %param.28) | copy-start | bytes 19972
  41.7 76.6 %copy-start.8 = (bf16[256,1664]{1,0:T(8,128)(2,1)S(1)}, bf16[256,1664]{1,0:T(8,128)(2,1)}, u32[]{:S(2)}) copy-start(bf16[256,1664]{1,0:T(8,128)(2,1)} %param.32) | copy-start | bytes 2555908
  41.7 76.6 %copy-start.10 = (f32[256]{0:T(256)S(1)}, f32[256]{0:T(256)}, u32[]{:S(2)}) copy-start(f32[256]{0:T(256)} %param.31) | copy-start | bytes 3076
  41.7 136.9 %reduce-scatter.5.cloned.1.call-start = ((), (), s32[]{:S(2)}) async-start(), calls=%async_computation.4 | async-start | bytes 905216 | tf_op jit(solution)/shard_map/reduce_scatter | solution.py:129
  118.3 4.1 %copy-start.11 = (s32[1,256]{1,0:T(1,128)S(1)}, s32[1,256]{1,0:T(1,128)}, u32[]{:S(2)}) copy-start(s32[1,256]{1,0:T(1,128)} %param.20) | copy-start | bytes 3076
  118.3 4.5 %copy-start.12 = (s32[1,32]{1,0:T(1,128)S(1)}, s32[1,32]{1,0:T(1,128)}, u32[]{:S(2)}) copy-start(s32[1,32]{1,0:T(1,128)} %param.21) | copy-start | bytes 388
  118.3 60.3 %copy-start.5 = (f32[1664]{0:T(1024)S(1)}, f32[1664]{0:T(1024)}, u32[]{:S(2)}) copy-start(f32[1664]{0:T(1024)} %param.33) | copy-start | bytes 19972
  179.4 20.3 %copy-start.7 = (f32[104]{0:T(128)S(1)}, f32[104]{0:T(128)}, u32[]{:S(2)}) copy-start(f32[104]{0:T(128)} %param.35) | copy-start | bytes 1252
Sparse Core Ops, SparseCore 0:
  41.8 55.1 reduce-scatter.2
  122.4 56.1 reduce-scatter.4
where the time goes:
time: 227 us; the launch traced here: 226 us
  waiting for transfers between devices  111 us (49%)
  blocking collectives  85.1 us (37%)
  between operations  13.6 us (6%)
  matrix products  8.37 us (4%)
  other arithmetic  6.89 us (3%)
    reduce_scatter x1, waiting for transfers between devices, on_device(): lax.psum_scatter(jnp.dot(block, down_weight, preferred_element_type=jnp.f...  55.7 us
    reduce_scatter x1, waiting for transfers between devices, on_device(): lax.psum_scatter(jnp.einsum('qhe,hed->qd', block, output_weight, preferre...  55.2 us
    all_gather x1, blocking collectives, on_device(): lax.all_gather(normed, 'grp', axis=0, tiled=True)  26.8 us
    all_gather x1, blocking collectives, on_device(): lax.all_gather(windows, 'grp', axis=0, tiled=True)  20.1 us
    all_gather x1, blocking collectives, on_device(): lax.all_gather(normed_again, 'grp', axis=0, tiled=True)  20.1 us
    all_to_all x1, blocking collectives, on_device(): lax.all_to_all(outgoing, 'tok', split_axis=0, concat_axis=0, tiled=True)  18.1 us
  transfers between devices with their start and end apart: 2, of which 2 were waited for; matrix products, arithmetic and copies ran while one was open for 0% of the time, Pallas kernels for 0%

commit v1 on v0

--- a/solution.py
+++ b/solution.py
@@ -44,6 +44,15 @@
     return jnp.einsum(
         "hqk,khe->qhe", probabilities, value_rows, preferred_element_type=jnp.float32
     ).astype(jnp.bfloat16)
+
+
+def summed_apart(terms):
+    shards = lax.psum(1, "grp")
+    rows = terms.shape[0] // shards
+    pieces = lax.all_to_all(
+        terms.reshape(shards, rows, terms.shape[1]), "grp", 0, 0, tiled=False
+    )
+    return jnp.sum(pieces.astype(jnp.float32), axis=0)
 
 
 def routed_rows(merged, segments, live_rows, owners):
@@ -104,14 +113,11 @@
     projected = (lifted + input_shift[None]).astype(jnp.bfloat16)
     mixed = attend(projected, segments, live_rows, head_dim)
     block = mixed
-    attended = lax.psum_scatter(
+    attended = summed_apart(
         jnp.einsum("qhe,hed->qd", block, output_weight, preferred_element_type=jnp.float32).astype(
             jnp.bfloat16
-        ),
-        "grp",
-        scatter_dimension=0,
-        tiled=True,
-    ).astype(jnp.float32)
+        )
+    )
     residual = (stream.astype(jnp.float32) + attended + output_shift).astype(jnp.bfloat16)
     normed_again = normalize(residual.astype(jnp.float32), second_gain, second_shift).astype(
         jnp.bfloat16
@@ -126,12 +132,9 @@
     )
     activated = jax.nn.gelu(lifted, approximate=False).astype(jnp.bfloat16)
     block = activated
-    fed = lax.psum_scatter(
-        jnp.dot(block, down_weight, preferred_element_type=jnp.float32).astype(jnp.bfloat16),
-        "grp",
-        scatter_dimension=0,
-        tiled=True,
-    ).astype(jnp.float32)
+    fed = summed_apart(
+        jnp.dot(block, down_weight, preferred_element_type=jnp.float32).astype(jnp.bfloat16)
+    )
     layer_out = (residual.astype(jnp.float32) + fed + down_shift).astype(jnp.bfloat16)
     windows = layer_out.reshape(row_count // 4, 4 * model_width)
     merged = (

time: 227 us -> 151 us (0.67)
  waiting for transfers between devices: 111 us -> 23.3 us
  blocking collectives: 85.1 us -> 106 us
  between operations: 13.6 us -> 0.24 us
  starting transfers between devices: 0.04 us -> 5.33 us
    reduce_scatter x2 -> x0, waiting for transfers between devices: 111 us -> none  [the longest x1 55.7 us: on_device(): lax.psum_scatter(jnp.dot(block, down_weight, preferred_element_type=jnp.f...]
    all_to_all x0 -> x1, blocking collectives: none -> 27.1 us  [summed_apart(): lax.all_to_all(terms.reshape(shards, rows, terms.shape[1]), 'grp', 0, 0,...]
    all_to_all x0 -> x1, waiting for transfers between devices: none -> 23.3 us  [summed_apart(): lax.all_to_all(terms.reshape(shards, rows, terms.shape[1]), 'grp', 0, 0,...]
    all_to_all x0 -> x1, starting transfers between devices: none -> 5.33 us  [summed_apart(): lax.all_to_all(terms.reshape(shards, rows, terms.shape[1]), 'grp', 0, 0,...]
    all_gather x1, blocking collectives: 20.1 us -> 16.8 us  [on_device(): lax.all_gather(windows, 'grp', axis=0, tiled=True)]
    all_gather x1, blocking collectives: 20.1 us -> 16.8 us  [on_device(): lax.all_gather(normed_again, 'grp', axis=0, tiled=True)]
  transfers between devices with their start and end apart: 2 -> 1, of which waited for: 2 -> 1; matrix products, arithmetic and copies ran while one was open for 0% -> 0% of each run, Pallas kernels for 0% -> 0%
where the time goes in v1:
time: 151 us; the launch traced here: 150 us
  blocking collectives  106 us (70%)
  waiting for transfers between devices  23.3 us (15%)
  matrix products  8.35 us (6%)
  other arithmetic  5.57 us (4%)
  starting transfers between devices  5.33 us (4%)
    all_to_all x1, blocking collectives, summed_apart(): lax.all_to_all(terms.reshape(shards, rows, terms.shape[1]), 'grp', 0, 0,...  27.1 us
    all_gather x1, blocking collectives, on_device(): lax.all_gather(normed, 'grp', axis=0, tiled=True)  26.8 us
    all_to_all x1, waiting for transfers between devices, summed_apart(): lax.all_to_all(terms.reshape(shards, rows, terms.shape[1]), 'grp', 0, 0,...  23.3 us
    all_to_all x1, blocking collectives, on_device(): lax.all_to_all(outgoing, 'tok', split_axis=0, concat_axis=0, tiled=True)  18.3 us
    all_gather x1, blocking collectives, on_device(): lax.all_gather(normed_again, 'grp', axis=0, tiled=True)  16.8 us
    all_gather x1, blocking collectives, on_device(): lax.all_gather(windows, 'grp', axis=0, tiled=True)  16.8 us
    all_to_all x1, starting transfers between devices, summed_apart(): lax.all_to_all(terms.reshape(shards, rows, terms.shape[1]), 'grp', 0, 0,...  5.33 us
    dot_general x1, matrix products, on_device(): jnp.dot(block, down_weight, preferred_element_type=jnp.float32)  3.89 us
  transfers between devices with their start and end apart: 1, of which 1 were waited for; matrix products, arithmetic and copies ran while one was open for 0% of the time, Pallas kernels for 0%

profile of v1, /device:TPU:1, one launch (start us, length us, event | category | flops | bytes accessed | tf_op | source)
XLA Modules:
  0.0 150.0 jit_solution(17663337159343310800)
XLA Ops:
  0.0 0.0 copy-start
  0.0 1.0 convert_reduce_fusion.3
  1.1 1.0 multiply_reduce_fusion
  2.1 0.9 add_convert_fusion.2
  3.0 0.0 copy-start.6
  3.0 26.8 %all_gather.9 = bf16[256,1664]{1,0:T(8,128)(2,1)S(1)} all-gather(bf16[16,1664]{1,0:T(8,128)(2,1)S(1)} %add_convert_fusion.2), channel_id=1, replica_groups=mesh['grp'=16,'tok'=32] {'grp'}, dimensions={0}, use_global_device_ids=true | all-gather | bytes 905216 | tf_op jit(solution)/shard_map/all_gather | solution.py:109
  29.8 0.7 compare_reduce_fusion
  30.5 0.7 reduce.5
  31.2 1.7 %fusion.2 = bf16[256,1,312]{0,2,1:T(8,128)(2,1)S(1)} fusion(bf16[256,1664]{1,0:T(8,128)(2,1)S(1)} %all_gather.9, bf16[1664,1,312]{0,2,1:T(8,128)(2,1)} %param.24, f32[312]{0:T(512)S(1)} %reduce.5), kind=kOutput, calls=%fused_computation.9 | convolution fusion | flops 265973760 | bytes 2051296 | tf_op jit(solution)/shard_map/sd,dhe->she/dot_general | solution.py:107
  33.0 0.0 copy-done.6
  33.0 0.3 fusion.106
  33.2 0.2 fusion.18
  33.4 1.7 %convolution_convert_fusion.1 = bf16[256,1664]{1,0:T(8,128)(2,1)S(1)} fusion(bf16[1,104,1664]{2,1,0:T(8,128)(2,1)} %param.26, f32[256,256]{0,1:T(8,128)S(1)} %get-tuple-element.8, f32[256]{0:T(256)S(1)} %fusion.18, f32[256]{0:T(256)S(1)} %get-tuple-element.7, s32[256]{0:T(256)S(1)} %bitcast.62, pred[256]{0:T(512)(128)(4,1)S(1)} %compare_reduce_fusion, ...), kind=kOutput, calls=%fused_computation.1 | convolution fusion | flops 103213056 | bytes 1518080 | tf_op jit(solution)/shard_map/qhe,hed->qd/dot_general | solution.py:117
  35.1 0.0 copy-start.1
  35.1 0.0 copy-start.2
  35.1 0.0 copy-start.4
  35.1 0.0 copy-start.5
  35.1 27.1 %all_to_all.15 = bf16[16,16,1664]{2,1,0:T(8,128)(2,1)S(1)} all-to-all(bf16[16,16,1664]{2,1,0:T(8,128)(2,1)S(1)} %bitcast.57), channel_id=1, replica_groups=mesh['grp'=16,'tok'=32] {'grp'}, dimensions={0} | all-to-all | bytes 1703936 | tf_op jit(solution)/shard_map/all_to_all | solution.py:52
  62.2 0.0 copy-start.8
  62.2 0.0 copy-start.9
  62.2 0.1 convert_reduce_fusion.1
  62.3 0.0 copy-done.1
  62.3 0.0 copy-done.2
  62.3 0.1 convert_reduce_fusion.2
  62.5 0.2 fusion.60
  62.7 0.0 copy-done.4
  62.7 0.0 copy-done.5
  62.7 0.1 fusion.63
  62.8 16.8 %all_gather.10 = bf16[256,1664]{1,0:T(8,128)(2,1)S(1)} all-gather(bf16[16,1664]{1,0:T(8,128)(2,1)S(1)} %fusion.63), channel_id=1, replica_groups=mesh['grp'=16,'tok'=32] {'grp'}, dimensions={0}, use_global_device_ids=true | all-gather | bytes 905216 | tf_op jit(solution)/shard_map/all_gather | solution.py:127
  79.6 0.0 copy-done.8
  79.6 0.0 copy-done.9
  79.6 3.9 %convolution_convert_fusion = bf16[256,1664]{1,0:T(8,128)(2,1)} fusion(bf16[256,1664]{1,0:T(8,128)(2,1)S(1)} %copy-done.8, bf16[256,1664]{1,0:T(8,128)(2,1)S(1)} %all_gather.10, bf16[1664,256]{1,0:T(8,128)(2,1)} %param.30, f32[256]{0:T(256)S(1)} %copy-done.9), kind=kOutput, calls=%fused_computation | convolution fusion | flops 440958976 | bytes 3408896 | tf_op jit(solution)/shard_map/dot_general | solution.py:136
  83.5 0.0 copy-start.3
  83.5 0.0 copy-start.10
  83.5 0.0 copy-start.11
  83.5 5.3 %all-to-all-start.1 = ((bf16[16,16,1664]{2,1,0:T(8,128)(2,1)}), bf16[16,16,1664]{2,1,0:T(8,128)(2,1)S(1)}, u32[]{:S(2)}, u32[]{:S(2)}) async-start(bf16[16,16,1664]{2,1,0:T(8,128)(2,1)} %bitcast.14), calls=%async_computation.1 | async-start | bytes 1703936 | tf_op jit(solution)/shard_map/all_to_all | solution.py:52
  88.9 0.2 slice.15
  89.1 0.0 copy-done.3
  89.1 0.0 copy-done.10
  89.1 0.2 slice.16
  89.3 0.2 convert_reduce_fusion.4
  89.4 0.0 copy-done.11
  89.5 0.1 select_reduce_fusion
  89.6 23.3 %all-to-all-done.1 = bf16[16,16,1664]{2,1,0:T(8,128)(2,1)S(1)} async-done(((bf16[16,16,1664]{2,1,0:T(8,128)(2,1)}), bf16[16,16,1664]{2,1,0:T(8,128)(2,1)S(1)}, u32[]{:S(2)}, u32[]{:S(2)}) %all-to-all-start.1) | async-done | bytes 852000 | tf_op jit(solution)/shard_map/all_to_all | solution.py:52
  112.9 0.1 convert_reduce_fusion
  113.0 0.1 fusion.68
  113.1 0.0 copy-start.7
  113.1 16.8 %all-gather = bf16[16,4,6656]{2,1,0:T(4,128)(2,1)S(1)} all-gather(bf16[1,4,6656]{2,1,0:T(4,128)(2,1)S(1)} %fusion.68), channel_id=1, replica_groups=mesh['grp'=16,'tok'=32] {'grp'}, dimensions={0}, use_global_device_ids=true | all-gather | bytes 905216 | tf_op jit(solution)/shard_map/all_gather | solution.py:142
  129.9 0.2 reshape.118
  130.1 0.0 copy-done
  130.1 0.0 copy-done.7
  130.2 0.8 convolution_convert_fusion.2
  131.0 0.1 copy.26
  131.1 18.3 %all_to_all.16 = bf16[32,8,104]{2,1,0:T(8,128)(2,1)S(1)} all-to-all(bf16[32,8,104]{2,1,0:T(8,128)(2,1)S(1)} %bitcast.58), channel_id=1, replica_groups=mesh['grp'=16,'tok'=32] {'tok'}, dimensions={0} | all-to-all | bytes 106496 | tf_op jit(solution)/shard_map/all_to_all | solution.py:149
  149.4 0.6 copy.29
  (13 shorter events, 0.2 us)
Async XLA Ops:
  0.0 130.1 %copy-start = (bf16[6656,104]{0,1:T(8,128)(2,1)S(1)}, bf16[6656,104]{0,1:T(8,128)(2,1)}, u32[]{:S(2)}) copy-start(bf16[6656,104]{0,1:T(8,128)(2,1)} %param.34) | copy-start | bytes 4153348
  3.0 30.0 %copy-start.6 = (s32[1,256]{1,0:T(1,128)S(1)}, s32[1,256]{1,0:T(1,128)}, u32[]{:S(2)}) copy-start(s32[1,256]{1,0:T(1,128)} %param.19) | copy-start | bytes 3076
  35.1 27.2 %copy-start.1 = (bf16[1,16,1664]{2,1,0:T(8,128)(2,1)S(1)}, bf16[1,16,1664]{2,1,0:T(8,128)(2,1)}, u32[]{:S(2)}) copy-start(bf16[1,16,1664]{2,1,0:T(8,128)(2,1)} %param.18) | copy-start | bytes 159748
  35.1 27.2 %copy-start.2 = (f32[1664]{0:T(1024)S(1)}, f32[1664]{0:T(1024)}, u32[]{:S(2)}) copy-start(f32[1664]{0:T(1024)} %param.27) | copy-start | bytes 19972
  35.1 27.6 %copy-start.4 = (f32[1664]{0:T(1024)S(1)}, f32[1664]{0:T(1024)}, u32[]{:S(2)}) copy-start(f32[1664]{0:T(1024)} %param.29) | copy-start | bytes 19972
  35.1 27.6 %copy-start.5 = (f32[1664]{0:T(1024)S(1)}, f32[1664]{0:T(1024)}, u32[]{:S(2)}) copy-start(f32[1664]{0:T(1024)} %param.28) | copy-start | bytes 19972
  62.2 17.4 %copy-start.8 = (bf16[256,1664]{1,0:T(8,128)(2,1)S(1)}, bf16[256,1664]{1,0:T(8,128)(2,1)}, u32[]{:S(2)}) copy-start(bf16[256,1664]{1,0:T(8,128)(2,1)} %param.32) | copy-start | bytes 2555908
  62.2 17.4 %copy-start.9 = (f32[256]{0:T(256)S(1)}, f32[256]{0:T(256)}, u32[]{:S(2)}) copy-start(f32[256]{0:T(256)} %param.31) | copy-start | bytes 3076
  83.5 5.6 %copy-start.3 = (f32[1664]{0:T(1024)S(1)}, f32[1664]{0:T(1024)}, u32[]{:S(2)}) copy-start(f32[1664]{0:T(1024)} %param.33) | copy-start | bytes 19972
  83.5 5.6 %copy-start.10 = (s32[1,256]{1,0:T(1,128)S(1)}, s32[1,256]{1,0:T(1,128)}, u32[]{:S(2)}) copy-start(s32[1,256]{1,0:T(1,128)} %param.20) | copy-start | bytes 3076
  83.5 5.9 %copy-start.11 = (s32[1,32]{1,0:T(1,128)S(1)}, s32[1,32]{1,0:T(1,128)}, u32[]{:S(2)}) copy-start(s32[1,32]{1,0:T(1,128)} %param.21) | copy-start | bytes 388
  83.5 29.4 %all-to-all-start.1 = ((bf16[16,16,1664]{2,1,0:T(8,128)(2,1)}), bf16[16,16,1664]{2,1,0:T(8,128)(2,1)S(1)}, u32[]{:S(2)}, u32[]{:S(2)}) async-start(bf16[16,16,1664]{2,1,0:T(8,128)(2,1)} %bitcast.14), calls=%async_computation.1 | async-start | bytes 1703936 | tf_op jit(solution)/shard_map/all_to_all | solution.py:52
  113.1 17.0 %copy-start.7 = (f32[104]{0:T(128)S(1)}, f32[104]{0:T(128)}, u32[]{:S(2)}) copy-start(f32[104]{0:T(128)} %param.35) | copy-start | bytes 1252

commit v2 on v1

--- a/solution.py
+++ b/solution.py
@@ -38,8 +38,8 @@
     scores = jnp.einsum(
         "qhe,khe->hqk", queries, key_rows, preferred_element_type=jnp.float32
     ) * head_dim ** (-0.5)
-    probabilities = softmax_rows(scores, attention_mask(segments, live_rows)[None]).astype(
-        jnp.bfloat16
+    probabilities = lax.optimization_barrier(
+        softmax_rows(scores, attention_mask(segments, live_rows)[None]).astype(jnp.bfloat16)
     )
     return jnp.einsum(
         "hqk,khe->qhe", probabilities, value_rows, preferred_element_type=jnp.float32
@@ -103,16 +103,17 @@
     segments = segment_ids[0]
     live_rows = padding[0]
     stream = patches[0]
-    normed = normalize(stream.astype(jnp.float32), first_gain, first_shift).astype(jnp.bfloat16)
+    gathered = lax.all_gather(stream, "grp", axis=0, tiled=True)
+    normed = normalize(gathered.astype(jnp.float32), first_gain, first_shift).astype(jnp.bfloat16)
     lifted = jnp.einsum(
         "sd,dhe->she",
-        lax.all_gather(normed, "grp", axis=0, tiled=True),
+        normed,
         input_weight,
         preferred_element_type=jnp.float32,
     )
     projected = (lifted + input_shift[None]).astype(jnp.bfloat16)
     mixed = attend(projected, segments, live_rows, head_dim)
-    block = mixed
+    block = lax.optimization_barrier(mixed)
     attended = summed_apart(
         jnp.einsum("qhe,hed->qd", block, output_weight, preferred_element_type=jnp.float32).astype(
             jnp.bfloat16
@@ -131,7 +132,7 @@
         + up_shift
     )
     activated = jax.nn.gelu(lifted, approximate=False).astype(jnp.bfloat16)
-    block = activated
+    block = lax.optimization_barrier(activated)
     fed = summed_apart(
         jnp.dot(block, down_weight, preferred_element_type=jnp.float32).astype(jnp.bfloat16)
     )

time: 151 us -> 144 us (0.954)
  matrix products: 8.35 us -> 4.68 us
  other arithmetic: 5.57 us -> 1.96 us
    dot_general x1, matrix products: 3.89 us -> 1.35 us  [on_device(): jnp.dot(block, down_weight, preferred_element_type=jnp.float32)]
where the time goes in v2:
time: 144 us
  blocking collectives  106 us (74%)
  waiting for transfers between devices  23.3 us (16%)
  starting transfers between devices  5.33 us (4%)
  matrix products  4.68 us (3%)
  other arithmetic  1.96 us (1%)
  local copies, waits for them, and re-layouts  1.85 us (1%)
    all_gather x1, blocking collectives, on_device(): gathered = lax.all_gather(stream, 'grp', axis=0, tiled=True)  27.2 us
    all_to_all x1, blocking collectives, summed_apart(): lax.all_to_all(terms.reshape(shards, rows, terms.shape[1]), 'grp', 0, 0,...  27 us
    all_to_all x1, waiting for transfers between devices, summed_apart(): lax.all_to_all(terms.reshape(shards, rows, terms.shape[1]), 'grp', 0, 0,...  23.3 us
    all_to_all x1, blocking collectives, on_device(): lax.all_to_all(outgoing, 'tok', split_axis=0, concat_axis=0, tiled=True)  18.3 us
    all_gather x1, blocking collectives, on_device(): lax.all_gather(normed_again, 'grp', axis=0, tiled=True)  16.8 us
    all_gather x1, blocking collectives, on_device(): lax.all_gather(windows, 'grp', axis=0, tiled=True)  16.8 us
    all_to_all x1, starting transfers between devices, summed_apart(): lax.all_to_all(terms.reshape(shards, rows, terms.shape[1]), 'grp', 0, 0,...  5.33 us
  transfers between devices with their start and end apart: 1, of which 1 were waited for; matrix products, arithmetic and copies ran while one was open for 0% of the time, Pallas kernels for 0%

profile of v2, /device:TPU:1, one launch (start us, length us, event | category | flops | bytes accessed | tf_op | source)
XLA Modules:
  0.0 143.6 jit_solution(7038068006779687679)
XLA Ops:
  0.0 0.0 copy-start
  0.0 0.0 copy-start.16
  0.0 0.0 copy-start.9
  0.0 0.0 copy-start.14
  0.0 0.0 copy-start.13
  0.0 0.0 copy-start.11
  0.0 27.2 %all-gather = bf16[1,256,1664]{2,1,0:T(8,128)(2,1)S(1)} all-gather(bf16[1,16,1664]{2,1,0:T(8,128)(2,1)} %param.18), channel_id=2, replica_groups=mesh['grp'=16,'tok'=32] {'grp'}, dimensions={1}, use_global_device_ids=true | all-gather | bytes 905216 | tf_op jit(solution)/shard_map/all_gather | solution.py:106
  27.2 0.2 convert_reduce_fusion
  27.5 0.4 fusion.3
  27.8 0.0 copy-done.16
  27.9 0.0 copy-done.9
  27.9 0.0 copy-done.14
  27.9 0.0 copy-done.13
  27.9 0.0 copy-done.11
  27.9 0.0 copy-start.5
  27.9 0.7 fusion.9
  28.6 0.0 copy-start.3
  28.6 0.0 copy-done.5
  28.6 0.3 fusion.50
  28.9 0.2 fusion.30
  29.1 0.1 fusion.32
  29.2 0.2 fusion.10
  29.4 0.2 copy-done.3
  29.6 0.4 convolution_convert_fusion.1
  30.0 0.0 copy-start.2
  30.1 0.0 copy-start.4
  30.1 0.0 copy-start.7
  30.1 0.0 copy-start.8
  30.1 27.0 %all_to_all.15 = bf16[16,16,1664]{2,1,0:T(8,128)(2,1)S(1)} all-to-all(bf16[16,16,1664]{2,1,0:T(8,128)(2,1)S(1)} %bitcast.72), channel_id=1, replica_groups=mesh['grp'=16,'tok'=32] {'grp'}, dimensions={0} | all-to-all | bytes 1703936 | tf_op jit(solution)/shard_map/all_to_all | solution.py:52
  57.1 0.0 copy-start.12
  57.1 0.0 copy-start.15
  57.1 0.1 convert_reduce_fusion.2
  57.3 0.0 copy-done.2
  57.3 0.0 copy-done.4
  57.3 0.1 convert_reduce_fusion.3
  57.4 0.2 fusion.35
  57.6 0.0 copy-done.7
  57.6 0.0 copy-done.8
  57.7 0.1 fusion.38
  57.7 16.8 %all_gather.10 = bf16[256,1664]{1,0:T(8,128)(2,1)S(1)} all-gather(bf16[16,1664]{1,0:T(8,128)(2,1)S(1)} %fusion.38), channel_id=1, replica_groups=mesh['grp'=16,'tok'=32] {'grp'}, dimensions={0}, use_global_device_ids=true | all-gather | bytes 905216 | tf_op jit(solution)/shard_map/all_gather | solution.py:128
  74.6 0.0 copy-done.12
  74.6 0.0 copy-done.15
  74.6 1.0 fusion.21
  75.6 0.2 copy-done.1
  75.7 1.4 convolution_convert_fusion
  77.1 5.3 %all-to-all-start.1 = ((bf16[16,16,1664]{2,1,0:T(8,128)(2,1)}), bf16[16,16,1664]{2,1,0:T(8,128)(2,1)S(1)}, u32[]{:S(2)}, u32[]{:S(2)}) async-start(bf16[16,16,1664]{2,1,0:T(8,128)(2,1)} %bitcast.17), calls=%async_computation.1 | async-start | bytes 1703936 | tf_op jit(solution)/shard_map/all_to_all | solution.py:52
  82.4 0.2 slice.15
  82.6 0.0 copy-done.6
  82.7 0.2 slice.16
  82.8 0.2 convert_reduce_fusion.4
  83.0 0.0 copy-done.17
  83.0 0.1 select_reduce_fusion
  83.2 23.3 %all-to-all-done.1 = bf16[16,16,1664]{2,1,0:T(8,128)(2,1)S(1)} async-done(((bf16[16,16,1664]{2,1,0:T(8,128)(2,1)}), bf16[16,16,1664]{2,1,0:T(8,128)(2,1)S(1)}, u32[]{:S(2)}, u32[]{:S(2)}) %all-to-all-start.1) | async-done | bytes 852000 | tf_op jit(solution)/shard_map/all_to_all | solution.py:52
  106.4 0.1 convert_reduce_fusion.1
  106.6 0.1 fusion.43
  106.7 0.0 copy-start.10
  106.7 16.8 %all-gather.1 = bf16[16,4,6656]{2,1,0:T(4,128)(2,1)S(1)} all-gather(bf16[1,4,6656]{2,1,0:T(4,128)(2,1)S(1)} %fusion.43), channel_id=1, replica_groups=mesh['grp'=16,'tok'=32] {'grp'}, dimensions={0}, use_global_device_ids=true | all-gather | bytes 905216 | tf_op jit(solution)/shard_map/all_gather | solution.py:143
  123.5 0.2 reshape.122
  123.7 0.0 copy-done
  123.7 0.0 copy-done.10
  123.7 0.8 convolution_convert_fusion.2
  124.5 0.1 copy.26
  124.7 18.3 %all_to_all.16 = bf16[32,8,104]{2,1,0:T(8,128)(2,1)S(1)} all-to-all(bf16[32,8,104]{2,1,0:T(8,128)(2,1)S(1)} %bitcast.73), channel_id=1, replica_groups=mesh['grp'=16,'tok'=32] {'tok'}, dimensions={0} | all-to-all | bytes 106496 | tf_op jit(solution)/shard_map/all_to_all | solution.py:150
  143.0 0.6 copy.29
  (18 shorter events, 0.2 us)
Async XLA Ops:
  0.0 123.7 %copy-start = (bf16[6656,104]{0,1:T(8,128)(2,1)S(1)}, bf16[6656,104]{0,1:T(8,128)(2,1)}, u32[]{:S(2)}) copy-start(bf16[6656,104]{0,1:T(8,128)(2,1)} %param.34) | copy-start | bytes 4153348
  0.0 27.8 %copy-start.16 = (s32[1,256]{1,0:T(1,128)S(1)}, s32[1,256]{1,0:T(1,128)}, u32[]{:S(2)}) copy-start(s32[1,256]{1,0:T(1,128)} %param.20) | copy-start | bytes 3076
  0.0 27.9 %copy-start.9 = (f32[1,312]{1,0:T(1,128)S(1)}, f32[1,312]{1,0:T(1,128)}, u32[]{:S(2)}) copy-start(f32[1,312]{1,0:T(1,128)} %param.25) | copy-start | bytes 3748
  0.0 27.9 %copy-start.14 = (f32[1664]{0:T(1024)S(1)}, f32[1664]{0:T(1024)}, u32[]{:S(2)}) copy-start(f32[1664]{0:T(1024)} %param.22) | copy-start | bytes 19972
  0.0 27.9 %copy-start.13 = (f32[1664]{0:T(1024)S(1)}, f32[1664]{0:T(1024)}, u32[]{:S(2)}) copy-start(f32[1664]{0:T(1024)} %param.23) | copy-start | bytes 19972
  0.0 27.9 %copy-start.11 = (bf16[1664,1,312]{0,2,1:T(8,128)(2,1)S(1)}, bf16[1664,1,312]{0,2,1:T(8,128)(2,1)}, u32[]{:S(2)}) copy-start(bf16[1664,1,312]{0,2,1:T(8,128)(2,1)} %param.24) | copy-start | bytes 3115012
  27.9 0.7 copy-start.5
  28.6 1.0 copy-start.3
  30.0 27.2 %copy-start.2 = (bf16[1,16,1664]{2,1,0:T(8,128)(2,1)S(1)}, bf16[1,16,1664]{2,1,0:T(8,128)(2,1)}, u32[]{:S(2)}) copy-start(bf16[1,16,1664]{2,1,0:T(8,128)(2,1)} %param.18) | copy-start | bytes 159748
  30.1 27.2 %copy-start.4 = (f32[1664]{0:T(1024)S(1)}, f32[1664]{0:T(1024)}, u32[]{:S(2)}) copy-start(f32[1664]{0:T(1024)} %param.27) | copy-start | bytes 19972
  30.1 27.6 %copy-start.7 = (f32[1664]{0:T(1024)S(1)}, f32[1664]{0:T(1024)}, u32[]{:S(2)}) copy-start(f32[1664]{0:T(1024)} %param.29) | copy-start | bytes 19972
  30.1 27.6 %copy-start.8 = (f32[1664]{0:T(1024)S(1)}, f32[1664]{0:T(1024)}, u32[]{:S(2)}) copy-start(f32[1664]{0:T(1024)} %param.28) | copy-start | bytes 19972
  57.1 17.4 %copy-start.12 = (bf16[1664,256]{1,0:T(8,128)(2,1)S(1)}, bf16[1664,256]{1,0:T(8,128)(2,1)}, u32[]{:S(2)}) copy-start(bf16[1664,256]{1,0:T(8,128)(2,1)} %param.30) | copy-start | bytes 2555908
  57.1 17.4 %copy-start.15 = (f32[256]{0:T(256)S(1)}, f32[256]{0:T(256)}, u32[]{:S(2)}) copy-start(f32[256]{0:T(256)} %param.31) | copy-start | bytes 3076
  74.6 1.2 copy-start.1
  77.1 5.6 %copy-start.6 = (f32[1664]{0:T(1024)S(1)}, f32[1664]{0:T(1024)}, u32[]{:S(2)}) copy-start(f32[1664]{0:T(1024)} %param.33) | copy-start | bytes 19972
  77.1 5.9 %copy-start.17 = (s32[1,32]{1,0:T(1,128)S(1)}, s32[1,32]{1,0:T(1,128)}, u32[]{:S(2)}) copy-start(s32[1,32]{1,0:T(1,128)} %param.21) | copy-start | bytes 388
  77.1 29.4 %all-to-all-start.1 = ((bf16[16,16,1664]{2,1,0:T(8,128)(2,1)}), bf16[16,16,1664]{2,1,0:T(8,128)(2,1)S(1)}, u32[]{:S(2)}, u32[]{:S(2)}) async-start(bf16[16,16,1664]{2,1,0:T(8,128)(2,1)} %bitcast.17), calls=%async_computation.1 | async-start | bytes 1703936 | tf_op jit(solution)/shard_map/all_to_all | solution.py:52
  106.7 17.0 %copy-start.10 = (f32[104]{0:T(128)S(1)}, f32[104]{0:T(128)}, u32[]{:S(2)}) copy-start(f32[104]{0:T(128)} %param.35) | copy-start | bytes 1252
